TPU v7x, 512 devices: a whole 4x4x16 slice. The times are simulated.
512 devices in a mesh: walker: 32 (over z, y_lo), orb: 16 (over x, y_hi, core).
Axes of the slice: x: 4, y: 4 (y_hi: 2, y_lo: 2; y = y_hi * 2 + y_lo), z: 16, core: 2. Of those that a mesh axis runs over, the one named last changes fastest.
Arguments:
- tile_index: int32 [32768], P('walker'), may hold values from 0 to 63
- weights: bfloat16 [32768, 64], P('walker'), may hold values from -0.75 to 0.75
- electron: int32 [32768], P('walker'), may hold values from 0 to 767
- strength: float32 [32768], P('walker'), may hold values from -1.5 to 1.5
- spline_table: bfloat16 [4096, 4096], P(None, 'orb'), may hold values from -6 to 6
- rotation: bfloat16 [4096, 768], P('orb'), may hold values from -0.09375 to 0.09375
- inverse: bfloat16 [32, 768, 768], P('walker', 'orb'), may hold values from -0.21875 to 0.21875
Outputs:
- ratios: float32 [32768], P(('walker', 'orb'))
- gradient: float32 [4096, 768], P('orb')
All inputs are finite; a program needn't handle non-finite values.
Results may differ from a plain program's by a relative error of at most 0.0042.
Values may be sent and summed in bfloat16 or wider, within the bound.
No kernel may reach another device: no remote copies, remote signals or barrier semaphores. Data moves between devices by JAX's collectives and lax.ppermute only.
A program may use at most 64 MiB of HBM per device.

v0:
```python
import jax
import jax.numpy as jnp
from jax import lax
from jax.sharding import PartitionSpec as P


def body(tile_index, weights, electron, strength, spline_table, rotation, inverse):
    points = tile_index.shape[0]
    coeffs = weights.shape[1]
    tiles_count = spline_table.shape[0] // coeffs
    shards = lax.axis_size("orb")
    own_rows = points // shards
    first_point = lax.axis_index("orb") * own_rows
    onehot = (tile_index[:, None] == jnp.arange(tiles_count, dtype=jnp.int32)[None, :]).astype(
        jnp.bfloat16
    )
    stencil_matrix = (onehot[:, :, None] * weights[:, None, :]).reshape(
        points, tiles_count * coeffs
    )
    orbital_values = jnp.dot(
        stencil_matrix, spline_table, preferred_element_type=jnp.float32
    ).astype(jnp.bfloat16)
    local_inverse = inverse[0]
    rotated = lax.psum_scatter(
        lax.dot_general(
            rotation, orbital_values, (((0,), (1,)), ((), ())), preferred_element_type=jnp.float32
        ),
        "orb",
        scatter_dimension=0,
        tiled=True,
    )
    columns = jnp.take(local_inverse, electron, axis=1).astype(jnp.float32)
    partial_ratio = jnp.sum(rotated * columns, axis=0)
    ratio_total = lax.psum(partial_ratio, "orb")
    ratios = lax.dynamic_slice_in_dim(ratio_total, first_point, own_rows, 0)
    adjoint = (columns * strength[None, :]).astype(jnp.bfloat16)
    local_gradient = lax.dot_general(
        orbital_values,
        lax.all_gather(adjoint, "orb", axis=0, tiled=True),
        (((0,), (1,)), ((), ())),
        preferred_element_type=jnp.float32,
    )
    gradient = lax.psum(local_gradient, "walker")
    return (ratios, gradient)


def solution(mesh):
    in_specs = (
        P("walker"),
        P("walker", None),
        P("walker"),
        P("walker"),
        P(None, "orb"),
        P("orb", None),
        P("walker", "orb", None),
    )
    out_specs = (P(("walker", "orb")), P("orb", None))
    return jax.shard_map(body, mesh=mesh, in_specs=in_specs, out_specs=out_specs, check_vma=False)
```

profile of v0, /device:TPU:4, one launch (start us, length us, event | category | flops | bytes accessed | tf_op | source)
XLA Modules:
  0.0 463.4 jit_solution(13601765400764669437)
XLA Ops:
  7.2 0.0 copy-start
  7.2 0.0 reduce-scatter.4.cloned.1.call-start
  7.2 0.9 fusion
  8.1 1.5 broadcast_multiply_fusion
  9.5 0.0 copy-done
  9.5 0.0 copy-start.1
  9.6 2.5 convolution_convert_fusion
  12.0 0.0 copy-done.1
  12.0 2.2 convolution_bitcast_fusion
  14.3 3.5 copy.17
  17.8 0.0 copy-start.2
  17.8 0.0 copy-start.3
  17.8 0.0 copy-start.4
  17.8 0.0 reduce-scatter.4.cloned.1.call-update
  17.8 0.0 all-gather.2.cloned.1.call-start
  17.9 0.8 copy-done.2
  18.7 0.2 copy.14
  18.8 0.0 copy-done.3
  18.9 3.2 gather_fusion
  22.1 0.1 copy.15
  22.2 97.2 %reduce-scatter.4.cloned.1.call-done = f32[48,1024]{1,0:T(8,128)} async-done(((f32[768,1024]{1,0:T(8,128)}), f32[48,1024]{1,0:T(8,128)}) %reduce-scatter.4.cloned.1.call-update) | async-done | bytes 196624 | tf_op jit(solution)/shard_map/reduce_scatter | solution.py:24
  119.4 0.0 copy-done.4
  119.4 1.6 fusion.2
  121.0 0.0 all-gather.2.cloned.1.call-update
  121.0 0.0 all-reduce.2.cloned.1.call-start
  121.1 62.9 %all-gather.2.cloned.1.call-done = bf16[768,1024]{1,0:T(8,128)(2,1)} async-done(((bf16[48,1024]{1,0:T(8,128)(2,1)}), bf16[768,1024]{1,0:T(8,128)(2,1)}) %all-gather.2.cloned.1.call-update) | async-done | bytes 1572880 | tf_op jit(solution)/shard_map/all_gather | solution.py:39
  184.0 2.9 fusion.4
  186.9 0.0 all-reduce.2.cloned.1.call-update
  187.0 30.3 %psum.14 = f32[1024]{0:T(1024)S(1)} all-reduce(f32[1024]{0:T(1024)S(1)} %get-tuple-element.3), channel_id=1, replica_groups=mesh['walker'=32,'orb'=16] {'orb'}, use_global_device_ids=true, to_apply=%region_2.3 | all-reduce | flops 1024 | bytes 8192 | tf_op jit(solution)/shard_map/psum | solution.py:34
  217.3 0.6 dynamic_slice.3
  217.8 237.0 %all-reduce.2.cloned.1.call-done = f32[256,768]{1,0:T(8,128)} async-done(((f32[256,768]{1,0:T(8,128)}), f32[256,768]{1,0:T(8,128)}) %all-reduce.2.cloned.1.call-update) | async-done | bytes 786448 | tf_op jit(solution)/shard_map/psum | solution.py:43
  454.8 2.1 copy.20
  (2 shorter events, 0.0 us)
Async XLA Ops:
  7.2 2.4 copy-start
  7.2 112.2 %reduce-scatter.4.cloned.1.call-start = ((), (), s32[]{:S(2)}) async-start(), calls=%async_computation.3 | async-start | bytes 3342336 | tf_op jit(solution)/shard_map/reduce_scatter | solution.py:24
  9.5 2.5 copy-start.1
  17.8 0.9 copy-start.2
  17.8 1.1 copy-start.3
  17.8 101.6 %copy-start.4 = (f32[1024]{0:T(1024)S(1)}, f32[1024]{0:T(1024)}, u32[]{:S(2)}) copy-start(f32[1024]{0:T(1024)} %param.10) | copy-start | bytes 12292
  17.8 166.2 %all-gather.2.cloned.1.call-start = ((), (), s32[]{:S(2)}) async-start(), calls=%async_computation.1 | async-start | bytes 1671168 | tf_op jit(solution)/shard_map/all_gather | solution.py:39
  121.0 333.8 %all-reduce.2.cloned.1.call-start = ((), (), s32[]{:S(2)}) async-start(), calls=%async_computation.2 | async-start | bytes 1572864 | tf_op jit(solution)/shard_map/psum | solution.py:43
Sparse Core Ops, SparseCore 0:
  17.9 101.4 reduce-scatter.3
  123.2 60.7 all-gather.1
  187.5 267.2 all-reduce.1
where the time goes:
time: 464 us; the launch traced here: 463 us
  waiting for transfers between devices  397 us (86%)
  blocking collectives  30.3 us (7%)
  between operations  13.8 us (3%)
  local copies, waits for them, and re-layouts  10.5 us (2%)
  matrix products  7.59 us (2%)
    psum x1, waiting for transfers between devices, body(): gradient = lax.psum(local_gradient, 'walker')  237 us
    reduce_scatter x1, waiting for transfers between devices, body(): lax.psum_scatter(lax.dot_general(rotation, orbital_values, (((0,), (1,)),...  97.2 us
    all_gather x1, waiting for transfers between devices, body(): lax.all_gather(adjoint, 'orb', axis=0, tiled=True)  62.9 us
    psum x1, blocking collectives, body(): ratio_total = lax.psum(partial_ratio, 'orb')  30.3 us
  transfers between devices with their start and end apart: 3, of which 3 were waited for; matrix products, arithmetic and copies ran while one was open for 1% of the time, Pallas kernels for 0%

commit v1 on v0

--- a/solution.py
+++ b/solution.py
@@ -36,7 +36,9 @@
     adjoint = (columns * strength[None, :]).astype(jnp.bfloat16)
     local_gradient = lax.dot_general(
         orbital_values,
-        lax.all_gather(adjoint, "orb", axis=0, tiled=True),
+        jnp.concatenate(
+            lax.all_to_all(jnp.stack([adjoint] * lax.axis_size("orb")), "orb", 0, 0), axis=0
+        ),
         (((0,), (1,)), ((), ())),
         preferred_element_type=jnp.float32,
     )

time: 464 us -> 424 us (0.914)
  waiting for transfers between devices: 397 us -> 333 us
  blocking collectives: 30.3 us -> 56.3 us
    all_gather x1 -> x0, waiting for transfers between devices: 62.9 us -> none  [body(): lax.all_gather(adjoint, 'orb', axis=0, tiled=True)]
    all_to_all x0 -> x1, blocking collectives: none -> 27.2 us  [body(): lax.all_to_all(jnp.stack([adjoint] * lax.axis_size('orb')), 'orb', 0, 0)]
  transfers between devices with their start and end apart: 3 -> 2, of which waited for: 3 -> 2; matrix products, arithmetic and copies ran while one was open for 1% -> 1% of each run, Pallas kernels for 0% -> 0%
where the time goes in v1:
time: 424 us
  waiting for transfers between devices  333 us (79%)
  blocking collectives  56.3 us (13%)
  between operations  14.1 us (3%)
  local copies, waits for them, and re-layouts  10.7 us (3%)
  matrix products  6.22 us (1%)
    psum x1, waiting for transfers between devices, body(): gradient = lax.psum(local_gradient, 'walker')  236 us
    reduce_scatter x1, waiting for transfers between devices, body(): lax.psum_scatter(lax.dot_general(rotation, orbital_values, (((0,), (1,)),...  97.2 us
    psum x1, blocking collectives, body(): ratio_total = lax.psum(partial_ratio, 'orb')  29.1 us
    all_to_all x1, blocking collectives, body(): lax.all_to_all(jnp.stack([adjoint] * lax.axis_size('orb')), 'orb', 0, 0)  27.2 us
  transfers between devices with their start and end apart: 2, of which 2 were waited for; matrix products, arithmetic and copies ran while one was open for 1% of the time, Pallas kernels for 0%

profile of v1, /device:TPU:4, one launch (start us, length us, event | category | flops | bytes accessed | tf_op | source)
XLA Modules:
  0.0 424.0 jit_solution(13199036812561367098)
XLA Ops:
  7.2 0.0 copy-start
  7.2 0.0 reduce-scatter.4.cloned.1.call-start
  7.2 0.9 fusion
  8.1 1.5 broadcast_multiply_fusion
  9.5 0.0 copy-done
  9.6 0.0 copy-start.1
  9.6 2.5 convolution_convert_fusion
  12.0 0.0 copy-done.1
  12.0 2.3 convolution_bitcast_fusion
  14.3 3.5 copy.19
  17.8 0.0 copy-start.2
  17.8 0.0 copy-start.3
  17.9 0.0 copy-start.4
  17.9 0.0 reduce-scatter.4.cloned.1.call-update
  17.9 0.0 all-reduce.2.cloned.1.call-start
  17.9 0.8 copy-done.2
  18.7 0.2 copy.16
  18.9 0.0 copy-done.3
  18.9 3.2 gather_fusion
  22.1 0.1 copy.17
  22.3 97.2 %reduce-scatter.4.cloned.1.call-done = f32[48,1024]{1,0:T(8,128)} async-done(((f32[768,1024]{1,0:T(8,128)}), f32[48,1024]{1,0:T(8,128)}) %reduce-scatter.4.cloned.1.call-update) | async-done | bytes 196624 | tf_op jit(solution)/shard_map/reduce_scatter | solution.py:24
  119.5 0.0 copy-done.4
  119.5 1.0 fusion.2
  120.4 0.2 stack.2
  120.6 27.2 %all_to_all.5 = bf16[16,48,1024]{2,1,0:T(8,128)(2,1)S(1)} all-to-all(bf16[16,48,1024]{2,1,0:T(8,128)(2,1)S(1)} %stack.2), channel_id=1, replica_groups=mesh['walker'=32,'orb'=16] {'orb'}, dimensions={0} | all-to-all | bytes 3145728 | tf_op jit(solution)/shard_map/all_to_all | solution.py:40
  147.8 1.5 fusion.4
  149.3 0.0 all-reduce.2.cloned.1.call-update
  149.3 29.1 %psum.14 = f32[1024]{0:T(1024)S(1)} all-reduce(f32[1024]{0:T(1024)S(1)} %get-tuple-element.3), channel_id=1, replica_groups=mesh['walker'=32,'orb'=16] {'orb'}, use_global_device_ids=true, to_apply=%region_2.3 | all-reduce | flops 1024 | bytes 8192 | tf_op jit(solution)/shard_map/psum | solution.py:34
  178.5 0.6 dynamic_slice.3
  179.0 236.0 %all-reduce.2.cloned.1.call-done = f32[256,768]{1,0:T(8,128)} async-done(((f32[256,768]{1,0:T(8,128)}), f32[256,768]{1,0:T(8,128)}) %all-reduce.2.cloned.1.call-update) | async-done | bytes 786448 | tf_op jit(solution)/shard_map/psum | solution.py:45
  415.1 2.1 copy.22
  (2 shorter events, 0.0 us)
Async XLA Ops:
  7.2 2.4 copy-start
  7.2 112.3 %reduce-scatter.4.cloned.1.call-start = ((), (), s32[]{:S(2)}) async-start(), calls=%async_computation.3 | async-start | bytes 3342336 | tf_op jit(solution)/shard_map/reduce_scatter | solution.py:24
  9.6 2.5 copy-start.1
  17.8 0.9 copy-start.2
  17.8 1.1 copy-start.3
  17.9 101.6 %copy-start.4 = (f32[1024]{0:T(1024)S(1)}, f32[1024]{0:T(1024)}, u32[]{:S(2)}) copy-start(f32[1024]{0:T(1024)} %param.10) | copy-start | bytes 12292
  17.9 397.2 %all-reduce.2.cloned.1.call-start = ((), (), s32[]{:S(2)}) async-start(), calls=%async_computation.2 | async-start | bytes 1572864 | tf_op jit(solution)/shard_map/psum | solution.py:45
Sparse Core Ops, SparseCore 0:
  18.0 101.4 reduce-scatter.3
  149.4 265.5 all-reduce.1
